TPU v7x, 32 devices: a whole 2x2x4 slice. The times are simulated.
32 devices in a mesh: visit: 4 (over z), row: 2 (over core), col: 4 (over y, x).
Axes of the slice: x: 2, y: 2, z: 4, core: 2. Of those that a mesh axis runs over, the one named last changes fastest.
Arguments:
- images: bfloat16 [16, 1024, 2048], P('visit', 'row', 'col'), may hold values from -10 to 10, as said below
- coeffs: float32 [16, 3], P('visit'), may hold values from 0.3 to 1.2
- pair_list: int32 [8, 3], replicated, may hold values from 0 to 480, as said below
- weights: bfloat16 [16, 2, 4], P('visit', 'row', 'col'), may hold values from 0.5 to 4
- resample_bank: bfloat16 [12, 512, 512], replicated, may hold values from -0.25 to 0.25
- warp_index: int32 [16, 2, 4, 2], P('visit', 'row', 'col'), may hold values from 0 to 11
- destinations: int32 [16, 2, 4, 4], P('visit', 'row', 'col'), may hold values from 0 to 3, as said below
- counts: int32 [16, 2, 4], P('visit', 'row', 'col'), may hold values from 3 to 4
Outputs:
- coadd_patch: float32 [4, 1024, 2048], P('visit', 'row', 'col')
- plane_fit: float32 [16, 3], P('visit')
Inputs may be any that keep to these rules, and one draw needn't show every extreme that they name: `images`: noise plus a per-exposure sky plane. `pair_list`: every exposure appears in exactly one pair; offsets lie in 0 to 480, both ends used. `destinations`: the used entries of one tile's list are distinct; each tile lists the patch of its own visit index; a patch drawn with skew, which may be the device's own visit patch, is listed by all 4 tiles at each device position.
All inputs are finite; a program needn't handle non-finite values.
Results may differ from a plain program's by a relative error of at most 0.015.
Values may be sent and summed in bfloat16 or wider, within the bound.
No kernel may reach another device: no remote copies, remote signals or barrier semaphores. Data moves between devices by JAX's collectives and lax.ppermute only.
A program may use at most 192 MiB of HBM per device.

v0:
```python
import jax
import jax.numpy as jnp
from jax import lax
from jax.sharding import PartitionSpec as P

HALO = 16
STRIP = 32
MAXD = 4
SIGMA_PARTS = (0.0625, 0.125, 0.25)


def extended(value, sides, width):
    for axis, dim in sides:
        devices, length = (lax.axis_size(axis), value.shape[dim])
        up = [(i, (i + 1) % devices) for i in range(devices - 1)]
        down = [(j, i) for i, j in up]
        last = lax.slice_in_dim(value, length - width, length, axis=dim)
        initial = lax.slice_in_dim(value, 0, width, axis=dim)
        before = lax.ppermute(last, axis, up)
        after = lax.ppermute(initial, axis, down)
        value = jnp.concatenate([before, value, after], axis=dim)
    return value


def band_table(length, width, sigma):
    spread = (jnp.arange(2 * width + 1) - width).astype(jnp.float32)
    curve = jnp.exp(-spread * spread / (2.0 * sigma * sigma))
    total = jnp.sum(curve)
    rows_grid = lax.broadcasted_iota(jnp.int32, (length, length + 2 * width), 0)
    cols_grid = lax.broadcasted_iota(jnp.int32, (length, length + 2 * width), 1)
    offset = (cols_grid - rows_grid - width).astype(jnp.float32)
    values = jnp.exp(-offset * offset / (2.0 * sigma * sigma)) / total
    return jnp.where(jnp.abs(offset) <= width, values, 0.0).astype(jnp.bfloat16)


def centred(index, length):
    return (index.astype(jnp.float32) + 0.5) / length * 2.0 - 1.0


def solve_three(normal, moments):
    lower = jnp.linalg.cholesky(normal)
    first = moments[..., 0] / lower[..., 0, 0]
    second = (moments[..., 1] - lower[..., 1, 0] * first) / lower[..., 1, 1]
    third = (moments[..., 2] - lower[..., 2, 0] * first - lower[..., 2, 1] * second) / lower[
        ..., 2, 2
    ]
    upper_top = third / lower[..., 2, 2]
    upper_mid = (second - lower[..., 2, 1] * upper_top) / lower[..., 1, 1]
    upper_low = (first - lower[..., 1, 0] * upper_mid - lower[..., 2, 0] * upper_top) / lower[
        ..., 0, 0
    ]
    return jnp.stack([upper_low, upper_mid, upper_top], -1)


def rows_from(source, anchor):
    return lax.dynamic_slice_in_dim(source, anchor, STRIP, 0)


def shards(images, coeffs, pair_list, weights, resample_bank, warp_index, destinations, counts):
    exp_dev = images.shape[0]
    tile_len = images.shape[1]
    row_count = lax.axis_size("row")
    col_count = lax.axis_size("col")
    visit_count = lax.axis_size("visit")
    row_pos = lax.axis_index("row")
    col_pos = lax.axis_index("col")
    visit_pos = lax.axis_index("visit")
    height = row_count * tile_len
    breadth = col_count * tile_len
    padded = extended(images, (("row", 1), ("col", 2)), HALO)
    matched = jnp.zeros((exp_dev, tile_len, tile_len), jnp.float32)
    for kernel in range(len(SIGMA_PARTS)):
        table = band_table(tile_len, HALO, HALO * SIGMA_PARTS[kernel])
        across = jnp.einsum(
            "ij,ejl->eil", table, padded, preferred_element_type=jnp.float32
        ).astype(jnp.bfloat16)
        smoothed = jnp.einsum("eil,ml->eim", across, table, preferred_element_type=jnp.float32)
        matched = matched + coeffs[:, kernel, None, None] * smoothed
    own_ids = visit_pos * exp_dev + jnp.arange(exp_dev, dtype=jnp.int32)
    first_col = pair_list[:, 0]
    second_col = pair_list[:, 1]
    offsets = pair_list[:, 2]
    hit_first = first_col[None, :] == own_ids[:, None]
    hit_second = second_col[None, :] == own_ids[:, None]
    partner = jnp.sum(
        jnp.where(hit_first, second_col[None, :], 0) + jnp.where(hit_second, first_col[None, :], 0),
        axis=1,
    )
    offset = jnp.sum(jnp.where(hit_first | hit_second, offsets[None, :], 0), axis=1)
    own_strip = jax.vmap(rows_from)(images, offset)
    everyone = lax.all_gather(own_strip, "visit", axis=0, tiled=True)
    theirs = jnp.take(everyone, partner, axis=0).astype(jnp.float32)
    nearby = jax.vmap(rows_from)(matched, offset)
    difference = nearby - theirs
    pixel_weight = 1.0 / (1.0 + theirs * theirs)
    strip_rows = row_pos * tile_len + offset[:, None] + jnp.arange(STRIP, dtype=jnp.int32)[None, :]
    ycoord = centred(strip_rows, height)[:, :, None]
    xcoord = centred(col_pos * tile_len + jnp.arange(tile_len, dtype=jnp.int32), breadth)
    xgrid = xcoord[None, None, :]
    weight_x = pixel_weight * xgrid
    weight_y = pixel_weight * ycoord
    sum_w = jnp.sum(pixel_weight, axis=(1, 2))
    sum_x = jnp.sum(weight_x, axis=(1, 2))
    sum_y = jnp.sum(weight_y, axis=(1, 2))
    sum_xx = jnp.sum(weight_x * xgrid, axis=(1, 2))
    sum_xy = jnp.sum(weight_x * ycoord, axis=(1, 2))
    sum_yy = jnp.sum(weight_y * ycoord, axis=(1, 2))
    normal = jnp.stack(
        [
            jnp.stack([sum_w, sum_x, sum_y], -1),
            jnp.stack([sum_x, sum_xx, sum_xy], -1),
            jnp.stack([sum_y, sum_xy, sum_yy], -1),
        ],
        1,
    )
    moments = jnp.stack(
        [
            jnp.sum(pixel_weight * difference, axis=(1, 2)),
            jnp.sum(weight_x * difference, axis=(1, 2)),
            jnp.sum(weight_y * difference, axis=(1, 2)),
        ],
        -1,
    )
    normal, moments = lax.psum((normal, moments), ("row", "col"))
    plane_fit = solve_three(normal, moments)
    row_coord = centred(row_pos * tile_len + jnp.arange(tile_len, dtype=jnp.int32), height)
    background = (
        plane_fit[:, 0, None, None]
        + plane_fit[:, 1, None, None] * xcoord[None, None, :]
        + plane_fit[:, 2, None, None] * row_coord[None, :, None]
    )
    corrected = (matched - background).astype(jnp.bfloat16)
    choose = warp_index[:, 0, 0, :]
    row_maps = jnp.take(resample_bank, choose[:, 0], axis=0)
    col_maps = jnp.take(resample_bank, choose[:, 1], axis=0)
    halfway = jnp.einsum(
        "eij,ejk->eik", row_maps, corrected, preferred_element_type=jnp.float32
    ).astype(jnp.bfloat16)
    warped = jnp.einsum(
        "eik,elk->eil", halfway, col_maps, preferred_element_type=jnp.float32
    ).astype(jnp.bfloat16)
    listed = destinations[:, 0, 0, :]
    how_many = counts[:, 0, 0]
    usable = jnp.arange(MAXD, dtype=jnp.int32)[None, :] < how_many[:, None]
    owners = jnp.arange(visit_count, dtype=jnp.int32)
    member = jnp.any(usable[:, :, None] & (listed[:, :, None] == owners[None, None, :]), axis=1)
    tile_weight = weights[:, 0, 0]
    nothing = jnp.zeros((), jnp.bfloat16)
    picked = jnp.where(member, tile_weight[:, None], nothing)
    partial_sum = jnp.einsum("ev,eij->vij", picked, warped, preferred_element_type=jnp.float32)
    partial_weight = jnp.sum(picked.astype(jnp.float32), axis=0)
    numerator, denominator = (
        lax.psum_scatter(
            partial_sum.astype(jnp.bfloat16), "visit", scatter_dimension=0, tiled=True
        ).astype(jnp.float32),
        lax.psum_scatter(
            partial_weight.astype(jnp.bfloat16), "visit", scatter_dimension=0, tiled=True
        ).astype(jnp.float32),
    )
    coadd_patch = numerator / denominator[:, None, None]
    return (coadd_patch, plane_fit)


def solution(mesh):
    in_specs = (
        P("visit", "row", "col"),
        P("visit", None),
        P(),
        P("visit", "row", "col"),
        P(),
        P("visit", "row", "col", None),
        P("visit", "row", "col", None),
        P("visit", "row", "col"),
    )
    out_specs = (P("visit", "row", "col"), P("visit", None))
    return jax.shard_map(shards, mesh=mesh, in_specs=in_specs, out_specs=out_specs, check_vma=False)
```

profile of v0, /device:TPU:0, one launch (start us, length us, event | category | flops | bytes accessed | tf_op | source)
XLA Modules:
  0.0 194.2 jit_solution(17051824752516389986)
XLA Ops:
  7.2 0.9 fusion.128
  8.1 1.0 copy.60
  9.1 2.4 %collective-permute-start = (bf16[4,16,512]{1,2,0:T(8,128)(2,1)}, bf16[4,16,512]{1,2,0:T(8,128)(2,1)S(1)}, u32[]{:S(2)}, u32[]{:S(2)}) collective-permute-start(bf16[4,16,512]{1,2,0:T(8,128)(2,1)} %copy.60), channel_id=1, source_target_pairs={{0,4},{1,5},{2,6},{3,7},{8,12},{9,13},{10,14},{11,15},{16,20},{17,... | collective-permute-start | bytes 196616 | tf_op jit(solution)/shard_map/ppermute | solution.py:19
  11.5 1.0 copy.61
  12.5 1.4 collective-permute-start.1
  13.9 4.2 %copy.62 = bf16[4,512,512]{1,2,0:T(8,128)(2,1)} copy(bf16[4,512,512]{2,1,0:T(8,128)(2,1)} %param.10) | data formatting | bytes 4194304 | tf_op args[0]
  18.7 0.6 exponential_reduce_fusion
  19.3 0.6 exponential_reduce_fusion.2
  19.9 2.9 %copy.63 = bf16[4,512,512]{2,0,1:T(4,128)(2,1)} copy(bf16[4,512,512]{2,1,0:T(8,128)(2,1)S(1)} %copy-done) | data formatting | bytes 4194304 | tf_op args[0]
  23.3 1.9 gather_fusion.1
  25.2 17.4 %all_gather.3 = bf16[16,32,512]{2,1,0:T(8,128)(2,1)S(1)} all-gather(bf16[4,32,512]{2,1,0:T(8,128)(2,1)S(1)} %copy.64), channel_id=1, replica_groups=mesh['visit'=4,'row'=2,'col'=4] {'visit'}, dimensions={0}, use_global_device_ids=true | all-gather | bytes 655360 | tf_op jit(solution)/shard_map/all_gather | solution.py:91
  42.7 4.8 %gather_fusion.3 = bf16[4,512,512]{2,1,0:T(8,128)(2,1)} fusion(bf16[12,512,512]{2,1,0:T(8,128)(2,1)} %param.14, s32[1024]{0:T(1024)S(1)} %get-tuple-element.65), kind=kCustom, calls=%fused_computation.clone | custom fusion | bytes 4194320 | tf_op jit(solution)/shard_map/jit(_take)/gather | solution.py:134
  47.5 5.0 %gather_fusion.4 = bf16[4,512,512]{2,1,0:T(8,128)(2,1)} fusion(bf16[12,512,512]{2,1,0:T(8,128)(2,1)} %param.14, s32[1024]{0:T(1024)S(1)} %get-tuple-element.64), kind=kCustom, calls=%fused_computation.1.clone | custom fusion | bytes 4194320 | tf_op jit(solution)/shard_map/jit(_take)/gather | solution.py:135
  53.3 0.9 pad_maximum_fusion.3
  54.1 3.4 %collective-permute-start.2 = (bf16[4,544,16]{1,2,0:T(8,128)(2,1)S(1)}, bf16[4,544,16]{1,2,0:T(8,128)(2,1)S(1)}, u32[]{:S(2)}, u32[]{:S(2)}) collective-permute-start(bf16[4,544,16]{1,2,0:T(8,128)(2,1)S(1)} %get-tuple-element.49), channel_id=1, source_target_pairs={{0,1},{1,2},{2,3},{4,5},{5,6},{6,7},{8,9},{9,10},{10,11},{12,13},{... | collective-permute-start | bytes 208904 | tf_op jit(solution)/shard_map/ppermute | solution.py:19
  57.5 1.5 collective-permute-start.3
  59.6 4.2 %collective-permute-done.3 = bf16[4,544,16]{1,2,0:T(8,128)(2,1)S(1)} collective-permute-done((bf16[4,544,16]{1,2,0:T(8,128)(2,1)S(1)}, bf16[4,544,16]{1,2,0:T(8,128)(2,1)S(1)}, u32[]{:S(2)}, u32[]{:S(2)}) %collective-permute-start.3) | collective-permute-done | bytes 69664 | tf_op jit(solution)/shard_map/ppermute | solution.py:20
  63.9 7.6 %fusion.2 = f32[4,512,512]{2,1,0:T(8,128)} fusion(f32[]{:T(128)} %exponential_reduce_fusion.1, bf16[4,544,16]{1,2,0:T(8,128)(2,1)S(1)} %collective-permute-done.3, bf16[4,16,512]{1,2,0:T(8,128)(2,1)} %collective-permute-done.1, bf16[4,512,512]{1,2,0:T(8,128)(2,1)S(1)} %copy-done.1, bf16[4,16,512]{1,2,0:T(8,128)(2,1)S(1)} %collective-permute-done, ...), kind=kOutput, calls=%fused_computation.10 | convolution fusion | flops 2372083712 | bytes 6561796 | tf_op jit(solution)/shard_map/eil,ml->eim/dot_general | solution.py:77
  71.4 7.7 %fusion = f32[4,512,512]{2,1,0:T(8,128)} fusion(f32[]{:T(128)} %exponential_reduce_fusion, bf16[4,544,16]{1,2,0:T(8,128)(2,1)S(1)} %collective-permute-done.3, bf16[4,16,512]{1,2,0:T(8,128)(2,1)} %collective-permute-done.1, bf16[4,512,512]{1,2,0:T(8,128)(2,1)S(1)} %copy-done.1, bf16[4,16,512]{1,2,0:T(8,128)(2,1)S(1)} %collective-permute-done, ...), kind=kOutput, calls=%fused_computation.8 | convolution fusion | flops 2372083712 | bytes 6561796 | tf_op jit(solution)/shard_map/eil,ml->eim/dot_general | solution.py:77
  79.1 9.8 %multiply_add_fusion = f32[4,512,512]{2,1,0:T(8,128)} fusion(f32[4,512,512]{2,1,0:T(8,128)} %fusion, f32[4,512,512]{2,1,0:T(8,128)} %fusion.2, f32[4]{0:T(128)S(1)} %get-tuple-element.30, f32[4]{0:T(128)S(1)} %get-tuple-element.31, f32[4]{0:T(128)S(1)} %get-tuple-element.29, f32[]{:T(128)} %exponential_reduce_fusion.2, ...), kind=kOutput, calls=%fused_computation.6 | convolution fusion | flops 2377326592 | bytes 14950452 | tf_op jit(solution)/shard_map/eil,ml->eim/dot_general | solution.py:77
  88.9 6.8 %copy.65 = f32[4,512,512]{2,0,1:T(4,128)} copy(f32[4,512,512]{2,1,0:T(8,128)} %multiply_add_fusion) | data formatting | bytes 8388608 | tf_op jit(solution)/shard_map/add | solution.py:78
  95.7 1.9 gather_fusion.2
  98.5 27.4 %all-reduce.2 = (f32[4,3,3]{1,2,0:T(4,128)S(1)}, f32[4,3]{0,1:T(4,128)S(1)}) all-reduce(f32[4,3,3]{1,2,0:T(4,128)S(1)} %pad_maximum_fusion.4, f32[4,3]{0,1:T(4,128)S(1)} %pad_maximum_fusion.5), channel_id=1, replica_groups=mesh['visit'=4,'row'=2,'col'=4] {'row','col'}, use_global_device_ids=true, to_apply=%region_16.18 | all-reduce | flops 48 | bytes 384 | tf_op jit(solution)/shard_map/psum | solution.py:124
  126.0 1.1 custom-call.4
  128.1 6.7 %fusion.22 = bf16[4,512,512]{2,1,0:T(8,128)(2,1)} fusion(bf16[4,512,512]{2,1,0:T(8,128)(2,1)} %gather_fusion.4, pred[4]{0:T(512)(128)(4,1)S(1)} %get-tuple-element.59, f32[4,512,512]{2,1,0:T(8,128)} %multiply_add_fusion, bf16[4,512,512]{2,1,0:T(8,128)(2,1)S(1)} %copy-done.2, f32[4,512]{1,0:T(4,128)S(1)} %get-tuple-element.67, ...), kind=kOutput, calls=%fused_computation.28 | convolution fusion | flops 2154823680 | bytes 10502152 | tf_op jit(solution)/shard_map/eik,elk->eil/dot_general | solution.py:139
  134.8 4.0 %fusion.27 = bf16[4,512,512]{2,0,1:T(4,128)(2,1)S(1)} fusion(bf16[4,512,512]{2,1,0:T(8,128)(2,1)} %fusion.22, pred[4,4]{1,0:T(4,128)(4,1)S(1)} %fusion.79, bf16[4]{0:T(256)(128)(2,1)S(1)} %bitcast.139), kind=kOutput, calls=%fused_computation.29 | convolution fusion | flops 9437200 | bytes 4194328 | tf_op jit(solution)/shard_map/ev,eij->vij/dot_general | solution.py:150
  138.8 1.8 copy.79
  140.7 11.5 %all-reduce.1 = bf16[4]{0:T(256)(128)(2,1)S(1)} all-reduce(bf16[4]{0:T(256)(128)(2,1)S(1)} %select_reduce_fusion.2), channel_id=3, replica_groups=mesh['visit'=4,'row'=2,'col'=4] {'visit'}, use_global_device_ids=true, to_apply=%region_21.23.clone | all-reduce | flops 4 | bytes 16
  152.8 1.2 dynamic-slice.1
  154.7 0.7 copy.80
  155.4 29.8 %reduce-scatter.2.cloned.1.call-done = bf16[1,512,512]{2,1,0:T(8,128)(2,1)} async-done(((bf16[4,512,512]{2,1,0:T(8,128)(2,1)}), bf16[1,512,512]{2,1,0:T(8,128)(2,1)}) %reduce-scatter.2.cloned.1.call-update) | async-done | bytes 524304 | tf_op jit(solution)/shard_map/reduce_scatter | solution.py:153
  185.2 2.2 %convert_divide_fusion = f32[1,512,512]{2,1,0:T(8,128)} fusion(bf16[1,512,512]{2,1,0:T(8,128)(2,1)} %reduce-scatter.2.cloned.1.call-done, f32[]{:T(128)S(6)} %convert.2), kind=kLoop, calls=%fused_computation.40 | loop fusion | flops 524288 | bytes 1572868 | tf_op jit(solution)/shard_map/div | solution.py:160
  (71 shorter events, 5.2 us)
Async XLA Ops:
  7.2 178.1 %reduce-scatter.2.cloned.1.call-start = ((), (), s32[]{:S(2)}) async-start(), calls=%async_computation.1 | async-start | bytes 2621440 | tf_op jit(solution)/shard_map/reduce_scatter | solution.py:153
  9.1 44.1 %collective-permute-start = (bf16[4,16,512]{1,2,0:T(8,128)(2,1)}, bf16[4,16,512]{1,2,0:T(8,128)(2,1)S(1)}, u32[]{:S(2)}, u32[]{:S(2)}) collective-permute-start(bf16[4,16,512]{1,2,0:T(8,128)(2,1)} %copy.60), channel_id=1, source_target_pairs={{0,4},{1,5},{2,6},{3,7},{8,12},{9,13},{10,14},{11,15},{16,20},{17,... | collective-permute-start | bytes 196616 | tf_op jit(solution)/shard_map/ppermute | solution.py:19
  12.5 7.4 %copy-start = (bf16[4,512,512]{2,1,0:T(8,128)(2,1)S(1)}, bf16[4,512,512]{2,1,0:T(8,128)(2,1)}, u32[]{:S(2)}) copy-start(bf16[4,512,512]{2,1,0:T(8,128)(2,1)} %param.10) | copy-start | bytes 6291460
  12.5 40.7 %collective-permute-start.1 = (bf16[4,16,512]{1,2,0:T(8,128)(2,1)}, bf16[4,16,512]{1,2,0:T(8,128)(2,1)}, u32[]{:S(2)}, u32[]{:S(2)}) collective-permute-start(bf16[4,16,512]{1,2,0:T(8,128)(2,1)} %copy.61), channel_id=1, source_target_pairs={{4,0},{5,1},{6,2},{7,3},{12,8},{13,9},{14,10},{15,11},{20,16},{21,... | collective-permute-start | bytes 196616 | tf_op jit(solution)/shard_map/ppermute | solution.py:20
  19.9 2.9 %copy-start.5 = (s32[8,3]{0,1:T(4,128)S(1)}, s32[8,3]{0,1:T(4,128)}, u32[]{:S(2)}) copy-start(s32[8,3]{0,1:T(4,128)} %param.12) | copy-start | bytes 292
  19.9 3.2 %copy-start.3 = (f32[4,3]{1,0:T(4,128)S(1)}, f32[4,3]{1,0:T(4,128)}, u32[]{:S(2)}) copy-start(f32[4,3]{1,0:T(4,128)} %param.11) | copy-start | bytes 148
  22.8 19.8 %copy-start.6 = (s32[4,1,1,2]{0,3,2,1:T(2,128)S(1)}, s32[4,1,1,2]{0,3,2,1:T(2,128)}, u32[]{:S(2)}) copy-start(s32[4,1,1,2]{0,3,2,1:T(2,128)} %param.15) | copy-start | bytes 100
  47.5 5.0 %copy-start.7 = (s32[4,1,1]{0,2,1:T(1,128)S(1)}, s32[4,1,1]{0,2,1:T(1,128)}, u32[]{:S(2)}) copy-start(s32[4,1,1]{0,2,1:T(1,128)} %param.17) | copy-start | bytes 52
  47.5 5.6 %copy-start.4 = (s32[4,1,1,4]{3,2,1,0:T(1,128)S(1)}, s32[4,1,1,4]{3,2,1,0:T(1,128)}, u32[]{:S(2)}) copy-start(s32[4,1,1,4]{3,2,1,0:T(1,128)} %param.16) | copy-start | bytes 196
  47.5 5.8 %copy-start.1 = (bf16[4,512,512]{1,2,0:T(8,128)(2,1)S(1)}, bf16[4,512,512]{1,2,0:T(8,128)(2,1)}, u32[]{:S(2)}) copy-start(bf16[4,512,512]{1,2,0:T(8,128)(2,1)} %copy.62) | copy-start | bytes 6291460
  54.1 5.5 %collective-permute-start.2 = (bf16[4,544,16]{1,2,0:T(8,128)(2,1)S(1)}, bf16[4,544,16]{1,2,0:T(8,128)(2,1)S(1)}, u32[]{:S(2)}, u32[]{:S(2)}) collective-permute-start(bf16[4,544,16]{1,2,0:T(8,128)(2,1)S(1)} %get-tuple-element.49), channel_id=1, source_target_pairs={{0,1},{1,2},{2,3},{4,5},{5,6},{6,7},{8,9},{9,10},{10,11},{12,13},{... | collective-permute-start | bytes 208904 | tf_op jit(solution)/shard_map/ppermute | solution.py:19
  57.5 6.3 %collective-permute-start.3 = (bf16[4,544,16]{1,2,0:T(8,128)(2,1)S(1)}, bf16[4,544,16]{1,2,0:T(8,128)(2,1)S(1)}, u32[]{:S(2)}, u32[]{:S(2)}) collective-permute-start(bf16[4,544,16]{1,2,0:T(8,128)(2,1)S(1)} %get-tuple-element.50), channel_id=1, source_target_pairs={{1,0},{2,1},{3,2},{5,4},{6,5},{7,6},{9,8},{10,9},{11,10},{13,12},{... | collective-permute-start | bytes 208904 | tf_op jit(solution)/shard_map/ppermute | solution.py:20
  95.7 32.4 %copy-start.2 = (bf16[4,512,512]{2,1,0:T(8,128)(2,1)S(1)}, bf16[4,512,512]{2,1,0:T(8,128)(2,1)}, u32[]{:S(2)}) copy-start(bf16[4,512,512]{2,1,0:T(8,128)(2,1)} %gather_fusion.3) | copy-start | bytes 6291460
  128.1 6.7 %copy-start.8 = (bf16[4,1,1]{0,2,1:T(2,128)(2,1)S(1)}, bf16[4,1,1]{0,2,1:T(2,128)(2,1)}, u32[]{:S(2)}) copy-start(bf16[4,1,1]{0,2,1:T(2,128)(2,1)} %param.13) | copy-start | bytes 28
  140.6 11.6 %copy-start.9 = (u32[32]{0:T(128)S(1)}, u32[32]{0:T(128)}, u32[]{:S(2)}) copy-start(u32[32]{0:T(128)} %constant.184) | copy-start | bytes 388
Sparse Core Ops, SparseCore 0:
  140.7 44.4 reduce-scatter.1
where the time goes:
time: 195 us; the launch traced here: 194 us
  blocking collectives  56.3 us (29%)
  local copies, waits for them, and re-layouts  36.1 us (19%)
  matrix products  35.7 us (18%)
  waiting for transfers between devices  34.7 us (18%)
  between operations  14.9 us (8%)
  starting transfers between devices  8.7 us (4%)
  other arithmetic  7.86 us (4%)
    reduce_scatter x1, waiting for transfers between devices, shards(): lax.psum_scatter(partial_sum.astype(jnp.bfloat16), 'visit', scatter_dimen...  29.8 us
    psum x1, blocking collectives, shards(): normal, moments = lax.psum((normal, moments), ('row', 'col'))  27.4 us
    dot_general x3, matrix products, shards(): jnp.einsum('eil,ml->eim', across, table, preferred_element_type=jnp.float32)  25 us
    all_gather x1, blocking collectives, shards(): everyone = lax.all_gather(own_strip, 'visit', axis=0, tiled=True)  17.4 us
    unnamed x1, blocking collectives  11.5 us
    unnamed x25, local copies, waits for them, and re-layouts  9.58 us
    add x1, local copies, waits for them, and re-layouts, shards(): matched = matched + coeffs[:, kernel, None, None] * smoothed  6.81 us
    dot_general x1, matrix products, shards(): jnp.einsum('eik,elk->eil', halfway, col_maps, preferred_element_type=jnp....  6.68 us
  transfers between devices with their start and end apart: 5, of which 3 were waited for; matrix products, arithmetic and copies ran while one was open for 13% of the time, Pallas kernels for 0%

commit v1 on v0

--- a/solution.py
+++ b/solution.py
@@ -121,7 +121,7 @@
         ],
         -1,
     )
-    normal, moments = lax.psum((normal, moments), ("row", "col"))
+    normal, moments = lax.psum(lax.psum((normal, moments), "col"), "row")
     plane_fit = solve_three(normal, moments)
     row_coord = centred(row_pos * tile_len + jnp.arange(tile_len, dtype=jnp.int32), height)
     background = (

time: 195 us -> 186 us (0.954)
  blocking collectives: 56.3 us -> 48 us
    psum x1 -> x2, blocking collectives: 27.4 us -> 19.2 us  [shards(): normal, moments = lax.psum(lax.psum((normal, moments), 'col'), 'row')]
  transfers between devices with their start and end apart: 5 -> 5, of which waited for: 3 -> 3; matrix products, arithmetic and copies ran while one was open for 13% -> 14% of each run, Pallas kernels for 0% -> 0%
where the time goes in v1:
time: 186 us; the launch traced here: 185 us
  blocking collectives  48 us (26%)
  local copies, waits for them, and re-layouts  36.1 us (19%)
  matrix products  35.7 us (19%)
  waiting for transfers between devices  34 us (18%)
  between operations  14.9 us (8%)
  starting transfers between devices  8.7 us (5%)
  other arithmetic  7.86 us (4%)
    reduce_scatter x1, waiting for transfers between devices, shards(): lax.psum_scatter(partial_sum.astype(jnp.bfloat16), 'visit', scatter_dimen...  29.2 us
    dot_general x3, matrix products, shards(): jnp.einsum('eil,ml->eim', across, table, preferred_element_type=jnp.float32)  25 us
    psum x2, blocking collectives, shards(): normal, moments = lax.psum(lax.psum((normal, moments), 'col'), 'row')  19.2 us
    all_gather x1, blocking collectives, shards(): everyone = lax.all_gather(own_strip, 'visit', axis=0, tiled=True)  17.4 us
    unnamed x1, blocking collectives  11.4 us
    unnamed x25, local copies, waits for them, and re-layouts  9.58 us
    add x1, local copies, waits for them, and re-layouts, shards(): matched = matched + coeffs[:, kernel, None, None] * smoothed  6.81 us
    dot_general x1, matrix products, shards(): jnp.einsum('eik,elk->eil', halfway, col_maps, preferred_element_type=jnp....  6.67 us
  transfers between devices with their start and end apart: 5, of which 3 were waited for; matrix products, arithmetic and copies ran while one was open for 14% of the time, Pallas kernels for 0%

profile of v1, /device:TPU:0, one launch (start us, length us, event | category | flops | bytes accessed | tf_op | source)
XLA Modules:
  0.0 185.3 jit_solution(7784702960893673501)
XLA Ops:
  7.2 0.9 fusion.128
  8.1 1.0 copy.60
  9.1 2.4 %collective-permute-start = (bf16[4,16,512]{1,2,0:T(8,128)(2,1)}, bf16[4,16,512]{1,2,0:T(8,128)(2,1)S(1)}, u32[]{:S(2)}, u32[]{:S(2)}) collective-permute-start(bf16[4,16,512]{1,2,0:T(8,128)(2,1)} %copy.60), channel_id=1, source_target_pairs={{0,4},{1,5},{2,6},{3,7},{8,12},{9,13},{10,14},{11,15},{16,20},{17,... | collective-permute-start | bytes 196616 | tf_op jit(solution)/shard_map/ppermute | solution.py:19
  11.5 1.0 copy.61
  12.5 1.4 collective-permute-start.1
  13.9 4.2 %copy.62 = bf16[4,512,512]{1,2,0:T(8,128)(2,1)} copy(bf16[4,512,512]{2,1,0:T(8,128)(2,1)} %param.10) | data formatting | bytes 4194304 | tf_op args[0]
  19.3 0.6 exponential_reduce_fusion.2
  19.9 2.9 %copy.63 = bf16[4,512,512]{2,0,1:T(4,128)(2,1)} copy(bf16[4,512,512]{2,1,0:T(8,128)(2,1)S(1)} %copy-done) | data formatting | bytes 4194304 | tf_op args[0]
  23.3 1.9 %gather_fusion.1 = bf16[4,32,512]{2,0,1:T(4,128)(2,1)S(1)} fusion(bf16[4,512,512]{2,0,1:T(4,128)(2,1)} %copy.63, s32[4]{0:T(128)S(1)} %fusion.95), kind=kCustom, calls=%fused_computation.3 | custom fusion | bytes 262192 | tf_op jit(solution)/shard_map/vmap()/gather | solution.py:56
  25.2 17.4 %all_gather.3 = bf16[16,32,512]{2,1,0:T(8,128)(2,1)S(1)} all-gather(bf16[4,32,512]{2,1,0:T(8,128)(2,1)S(1)} %copy.64), channel_id=1, replica_groups=mesh['visit'=4,'row'=2,'col'=4] {'visit'}, dimensions={0}, use_global_device_ids=true | all-gather | bytes 655360 | tf_op jit(solution)/shard_map/all_gather | solution.py:91
  42.7 4.8 %gather_fusion.3 = bf16[4,512,512]{2,1,0:T(8,128)(2,1)} fusion(bf16[12,512,512]{2,1,0:T(8,128)(2,1)} %param.14, s32[1024]{0:T(1024)S(1)} %get-tuple-element.67), kind=kCustom, calls=%fused_computation.clone | custom fusion | bytes 4194320 | tf_op jit(solution)/shard_map/jit(_take)/gather | solution.py:134
  47.5 5.0 %gather_fusion.4 = bf16[4,512,512]{2,1,0:T(8,128)(2,1)} fusion(bf16[12,512,512]{2,1,0:T(8,128)(2,1)} %param.14, s32[1024]{0:T(1024)S(1)} %get-tuple-element.66), kind=kCustom, calls=%fused_computation.1.clone | custom fusion | bytes 4194320 | tf_op jit(solution)/shard_map/jit(_take)/gather | solution.py:135
  53.3 0.9 pad_maximum_fusion.3
  54.1 3.4 %collective-permute-start.2 = (bf16[4,544,16]{1,2,0:T(8,128)(2,1)S(1)}, bf16[4,544,16]{1,2,0:T(8,128)(2,1)S(1)}, u32[]{:S(2)}, u32[]{:S(2)}) collective-permute-start(bf16[4,544,16]{1,2,0:T(8,128)(2,1)S(1)} %get-tuple-element.51), channel_id=1, source_target_pairs={{0,1},{1,2},{2,3},{4,5},{5,6},{6,7},{8,9},{9,10},{10,11},{12,13},{... | collective-permute-start | bytes 208904 | tf_op jit(solution)/shard_map/ppermute | solution.py:19
  57.5 1.5 collective-permute-start.3
  59.6 4.2 %collective-permute-done.3 = bf16[4,544,16]{1,2,0:T(8,128)(2,1)S(1)} collective-permute-done((bf16[4,544,16]{1,2,0:T(8,128)(2,1)S(1)}, bf16[4,544,16]{1,2,0:T(8,128)(2,1)S(1)}, u32[]{:S(2)}, u32[]{:S(2)}) %collective-permute-start.3) | collective-permute-done | bytes 69664 | tf_op jit(solution)/shard_map/ppermute | solution.py:20
  63.9 7.6 %fusion.2 = f32[4,512,512]{2,1,0:T(8,128)} fusion(f32[]{:T(128)} %exponential_reduce_fusion.1, bf16[4,544,16]{1,2,0:T(8,128)(2,1)S(1)} %collective-permute-done.3, bf16[4,16,512]{1,2,0:T(8,128)(2,1)} %collective-permute-done.1, bf16[4,512,512]{1,2,0:T(8,128)(2,1)S(1)} %copy-done.1, bf16[4,16,512]{1,2,0:T(8,128)(2,1)S(1)} %collective-permute-done, ...), kind=kOutput, calls=%fused_computation.10 | convolution fusion | flops 2372083712 | bytes 6561796 | tf_op jit(solution)/shard_map/eil,ml->eim/dot_general | solution.py:77
  71.4 7.7 %fusion = f32[4,512,512]{2,1,0:T(8,128)} fusion(f32[]{:T(128)} %exponential_reduce_fusion, bf16[4,544,16]{1,2,0:T(8,128)(2,1)S(1)} %collective-permute-done.3, bf16[4,16,512]{1,2,0:T(8,128)(2,1)} %collective-permute-done.1, bf16[4,512,512]{1,2,0:T(8,128)(2,1)S(1)} %copy-done.1, bf16[4,16,512]{1,2,0:T(8,128)(2,1)S(1)} %collective-permute-done, ...), kind=kOutput, calls=%fused_computation.8 | convolution fusion | flops 2372083712 | bytes 6561796 | tf_op jit(solution)/shard_map/eil,ml->eim/dot_general | solution.py:77
  79.1 9.8 %multiply_add_fusion = f32[4,512,512]{2,1,0:T(8,128)} fusion(f32[4,512,512]{2,1,0:T(8,128)} %fusion, f32[4,512,512]{2,1,0:T(8,128)} %fusion.2, f32[4]{0:T(128)S(1)} %get-tuple-element.30, f32[4]{0:T(128)S(1)} %get-tuple-element.31, f32[4]{0:T(128)S(1)} %get-tuple-element.29, f32[]{:T(128)} %exponential_reduce_fusion.2, ...), kind=kOutput, calls=%fused_computation.6 | convolution fusion | flops 2377326592 | bytes 14950452 | tf_op jit(solution)/shard_map/eil,ml->eim/dot_general | solution.py:77
  88.9 6.8 %copy.65 = f32[4,512,512]{2,0,1:T(4,128)} copy(f32[4,512,512]{2,1,0:T(8,128)} %multiply_add_fusion) | data formatting | bytes 8388608 | tf_op jit(solution)/shard_map/add | solution.py:78
  95.7 1.9 %gather_fusion.2 = f32[4,32,512]{2,0,1:T(4,128)S(1)} fusion(f32[4,512,512]{2,0,1:T(4,128)} %copy.65, s32[4]{0:T(128)S(1)} %fusion.95), kind=kCustom, calls=%fused_computation.4 | custom fusion | bytes 524336 | tf_op jit(solution)/shard_map/vmap()/gather | solution.py:56
  98.5 15.9 %all-reduce.2 = (f32[4,3,3]{1,2,0:T(4,128)S(1)}, f32[4,3]{0,1:T(4,128)S(1)}) all-reduce(f32[4,3,3]{1,2,0:T(4,128)S(1)} %pad_maximum_fusion.4, f32[4,3]{0,1:T(4,128)S(1)} %pad_maximum_fusion.5), channel_id=1, replica_groups=mesh['visit'=4,'row'=2,'col'=4] {'col'}, use_global_device_ids=true, to_apply=%region_17.19 | all-reduce | flops 48 | bytes 384 | tf_op jit(solution)/shard_map/psum | solution.py:124
  114.5 3.3 %all-reduce.3 = (f32[4,3,3]{1,2,0:T(4,128)S(1)}, f32[4,3]{0,1:T(4,128)S(1)}) all-reduce(f32[4,3,3]{1,2,0:T(4,128)S(1)} %get-tuple-element.34, f32[4,3]{0,1:T(4,128)S(1)} %get-tuple-element.35), channel_id=1, replica_groups=mesh['visit'=4,'row'=2,'col'=4] {'row'}, use_global_device_ids=true, to_apply=%region_18.20 | all-reduce | flops 48 | bytes 384 | tf_op jit(solution)/shard_map/psum | solution.py:124
  117.9 1.1 custom-call.4
  120.0 6.7 %fusion.22 = bf16[4,512,512]{2,1,0:T(8,128)(2,1)} fusion(bf16[4,512,512]{2,1,0:T(8,128)(2,1)} %gather_fusion.4, pred[4]{0:T(512)(128)(4,1)S(1)} %get-tuple-element.61, f32[4,512,512]{2,1,0:T(8,128)} %multiply_add_fusion, bf16[4,512,512]{2,1,0:T(8,128)(2,1)S(1)} %copy-done.2, f32[4,512]{1,0:T(4,128)S(1)} %get-tuple-element.69, ...), kind=kOutput, calls=%fused_computation.28 | convolution fusion | flops 2154823680 | bytes 10502152 | tf_op jit(solution)/shard_map/eik,elk->eil/dot_general | solution.py:139
  126.7 4.0 %fusion.27 = bf16[4,512,512]{2,0,1:T(4,128)(2,1)S(1)} fusion(bf16[4,512,512]{2,1,0:T(8,128)(2,1)} %fusion.22, pred[4,4]{1,0:T(4,128)(4,1)S(1)} %fusion.79, bf16[4]{0:T(256)(128)(2,1)S(1)} %bitcast.139), kind=kOutput, calls=%fused_computation.29 | convolution fusion | flops 9437200 | bytes 4194328 | tf_op jit(solution)/shard_map/ev,eij->vij/dot_general | solution.py:150
  130.6 1.8 copy.79
  132.5 11.4 %all-reduce.1 = bf16[4]{0:T(256)(128)(2,1)S(1)} all-reduce(bf16[4]{0:T(256)(128)(2,1)S(1)} %select_reduce_fusion.2), channel_id=3, replica_groups=mesh['visit'=4,'row'=2,'col'=4] {'visit'}, use_global_device_ids=true, to_apply=%region_23.25.clone | all-reduce | flops 4 | bytes 16
  144.5 1.2 dynamic-slice.1
  146.5 0.7 copy.80
  147.1 29.2 %reduce-scatter.2.cloned.1.call-done = bf16[1,512,512]{2,1,0:T(8,128)(2,1)} async-done(((bf16[4,512,512]{2,1,0:T(8,128)(2,1)}), bf16[1,512,512]{2,1,0:T(8,128)(2,1)}) %reduce-scatter.2.cloned.1.call-update) | async-done | bytes 524304 | tf_op jit(solution)/shard_map/reduce_scatter | solution.py:153
  176.3 2.2 %convert_divide_fusion = f32[1,512,512]{2,1,0:T(8,128)} fusion(bf16[1,512,512]{2,1,0:T(8,128)(2,1)} %reduce-scatter.2.cloned.1.call-done, f32[]{:T(128)S(6)} %convert.2), kind=kLoop, calls=%fused_computation.40 | loop fusion | flops 524288 | bytes 1572868 | tf_op jit(solution)/shard_map/div | solution.py:160
  (72 shorter events, 5.8 us)
Async XLA Ops:
  7.2 169.1 %reduce-scatter.2.cloned.1.call-start = ((), (), s32[]{:S(2)}) async-start(), calls=%async_computation.1 | async-start | bytes 2621440 | tf_op jit(solution)/shard_map/reduce_scatter | solution.py:153
  9.1 44.1 %collective-permute-start = (bf16[4,16,512]{1,2,0:T(8,128)(2,1)}, bf16[4,16,512]{1,2,0:T(8,128)(2,1)S(1)}, u32[]{:S(2)}, u32[]{:S(2)}) collective-permute-start(bf16[4,16,512]{1,2,0:T(8,128)(2,1)} %copy.60), channel_id=1, source_target_pairs={{0,4},{1,5},{2,6},{3,7},{8,12},{9,13},{10,14},{11,15},{16,20},{17,... | collective-permute-start | bytes 196616 | tf_op jit(solution)/shard_map/ppermute | solution.py:19
  12.5 7.4 %copy-start = (bf16[4,512,512]{2,1,0:T(8,128)(2,1)S(1)}, bf16[4,512,512]{2,1,0:T(8,128)(2,1)}, u32[]{:S(2)}) copy-start(bf16[4,512,512]{2,1,0:T(8,128)(2,1)} %param.10) | copy-start | bytes 6291460
  12.5 40.7 %collective-permute-start.1 = (bf16[4,16,512]{1,2,0:T(8,128)(2,1)}, bf16[4,16,512]{1,2,0:T(8,128)(2,1)}, u32[]{:S(2)}, u32[]{:S(2)}) collective-permute-start(bf16[4,16,512]{1,2,0:T(8,128)(2,1)} %copy.61), channel_id=1, source_target_pairs={{4,0},{5,1},{6,2},{7,3},{12,8},{13,9},{14,10},{15,11},{20,16},{21,... | collective-permute-start | bytes 196616 | tf_op jit(solution)/shard_map/ppermute | solution.py:20
  19.9 2.9 %copy-start.5 = (s32[8,3]{0,1:T(4,128)S(1)}, s32[8,3]{0,1:T(4,128)}, u32[]{:S(2)}) copy-start(s32[8,3]{0,1:T(4,128)} %param.12) | copy-start | bytes 292
  19.9 3.2 %copy-start.3 = (f32[4,3]{1,0:T(4,128)S(1)}, f32[4,3]{1,0:T(4,128)}, u32[]{:S(2)}) copy-start(f32[4,3]{1,0:T(4,128)} %param.11) | copy-start | bytes 148
  22.8 19.8 %copy-start.6 = (s32[4,1,1,2]{0,3,2,1:T(2,128)S(1)}, s32[4,1,1,2]{0,3,2,1:T(2,128)}, u32[]{:S(2)}) copy-start(s32[4,1,1,2]{0,3,2,1:T(2,128)} %param.15) | copy-start | bytes 100
  47.5 5.0 %copy-start.7 = (s32[4,1,1]{0,2,1:T(1,128)S(1)}, s32[4,1,1]{0,2,1:T(1,128)}, u32[]{:S(2)}) copy-start(s32[4,1,1]{0,2,1:T(1,128)} %param.17) | copy-start | bytes 52
  47.5 5.6 %copy-start.4 = (s32[4,1,1,4]{3,2,1,0:T(1,128)S(1)}, s32[4,1,1,4]{3,2,1,0:T(1,128)}, u32[]{:S(2)}) copy-start(s32[4,1,1,4]{3,2,1,0:T(1,128)} %param.16) | copy-start | bytes 196
  47.5 5.8 %copy-start.1 = (bf16[4,512,512]{1,2,0:T(8,128)(2,1)S(1)}, bf16[4,512,512]{1,2,0:T(8,128)(2,1)}, u32[]{:S(2)}) copy-start(bf16[4,512,512]{1,2,0:T(8,128)(2,1)} %copy.62) | copy-start | bytes 6291460
  54.1 5.5 %collective-permute-start.2 = (bf16[4,544,16]{1,2,0:T(8,128)(2,1)S(1)}, bf16[4,544,16]{1,2,0:T(8,128)(2,1)S(1)}, u32[]{:S(2)}, u32[]{:S(2)}) collective-permute-start(bf16[4,544,16]{1,2,0:T(8,128)(2,1)S(1)} %get-tuple-element.51), channel_id=1, source_target_pairs={{0,1},{1,2},{2,3},{4,5},{5,6},{6,7},{8,9},{9,10},{10,11},{12,13},{... | collective-permute-start | bytes 208904 | tf_op jit(solution)/shard_map/ppermute | solution.py:19
  57.5 6.3 %collective-permute-start.3 = (bf16[4,544,16]{1,2,0:T(8,128)(2,1)S(1)}, bf16[4,544,16]{1,2,0:T(8,128)(2,1)S(1)}, u32[]{:S(2)}, u32[]{:S(2)}) collective-permute-start(bf16[4,544,16]{1,2,0:T(8,128)(2,1)S(1)} %get-tuple-element.52), channel_id=1, source_target_pairs={{1,0},{2,1},{3,2},{5,4},{6,5},{7,6},{9,8},{10,9},{11,10},{13,12},{... | collective-permute-start | bytes 208904 | tf_op jit(solution)/shard_map/ppermute | solution.py:20
  95.7 24.3 %copy-start.2 = (bf16[4,512,512]{2,1,0:T(8,128)(2,1)S(1)}, bf16[4,512,512]{2,1,0:T(8,128)(2,1)}, u32[]{:S(2)}) copy-start(bf16[4,512,512]{2,1,0:T(8,128)(2,1)} %gather_fusion.3) | copy-start | bytes 6291460
  120.0 6.7 %copy-start.8 = (bf16[4,1,1]{0,2,1:T(2,128)(2,1)S(1)}, bf16[4,1,1]{0,2,1:T(2,128)(2,1)}, u32[]{:S(2)}) copy-start(bf16[4,1,1]{0,2,1:T(2,128)(2,1)} %param.13) | copy-start | bytes 28
  132.4 11.5 %copy-start.9 = (u32[32]{0:T(128)S(1)}, u32[32]{0:T(128)}, u32[]{:S(2)}) copy-start(u32[32]{0:T(128)} %constant.184) | copy-start | bytes 388
Sparse Core Ops, SparseCore 0:
  132.6 43.7 reduce-scatter.1
